TPU v7x, 512 devices: a whole 4x8x8 slice. The times are simulated.
512 devices in a mesh: dp: 32 (over y, x), tensor: 16 (over z, core).
Axes of the slice: x: 4, y: 8, z: 8, core: 2. Of those that a mesh axis runs over, the one named last changes fastest.
Arguments:
- patch_rows: bfloat16 [32, 3072, 1792], P('dp', 'tensor'), may hold values from -6 to 6
- send_rows: int32 [32, 16, 32, 6], P('dp', 'tensor'), may hold values from 0 to 192, as said below
- take_rows: int32 [32, 2048], P('dp', 'tensor'), may hold values from 0 to 191, as said below
- segments: int32 [32, 2048], P('dp', 'tensor'), may hold values from 0 to 41, never falling along the last dimension, each value on 1 to 96 neighbouring positions
- norm_gain: float32 [1792], replicated, may hold values from 0.5 to 5
- qkv_weight: bfloat16 [1792, 2688], P('tensor'), may hold values from -0.125 to 0.125
- out_weight: bfloat16 [896, 1792], P('tensor'), may hold values from -0.1875 to 0.1875
- grad_out: bfloat16 [32, 2048, 1792], P('dp', 'tensor'), may hold values from -6 to 6
Outputs:
- layer_out: bfloat16 [32, 2048, 1792], P('dp', 'tensor')
- patch_grad: bfloat16 [32, 3072, 1792], P('dp', 'tensor')
Inputs may be any that keep to these rules, and one draw needn't show every extreme that they name: `send_rows`: for each source device (s, t) the entries below 192 are distinct, 128 in all; for each group they fill slots from 0 on, the rest being 192; some device sends 6 rows to some group. `take_rows`: for each g and t the 128 entries are distinct and name exactly the slots s * 6 + c that hold a row (c below the number of rows that device (s, t) sends to group g). `segments`: along each row the ids never fall and each id covers 1 to 96 positions.
All inputs are finite; a program needn't handle non-finite values.
Results may differ from a plain program's by a relative error of at most 0.009.
The roundings to bfloat16 on the way count: a program that leaves them out, or rounds other values in their place, can miss the bound.
Values may be sent and summed in bfloat16 or wider, within the bound.
No kernel may reach another device: no remote copies, remote signals or barrier semaphores. Data moves between devices by JAX's collectives and lax.ppermute only.
A program may use at most 128 MiB of HBM per device.

v0:
```python
import jax
import jax.numpy as jnp
from jax import lax
from jax.sharding import PartitionSpec as P

HD = 112
HEADS = 8
MOST = 96


def extended(block, sides, width):
    for axis, dim in sides:
        count = lax.axis_size(axis)
        forward = [(i, i + 1) for i in range(count - 1)]
        backward = [(target, source) for source, target in forward]
        low = lax.ppermute(
            lax.slice_in_dim(block, block.shape[dim] - width, None, axis=dim), axis, forward
        )
        high = lax.ppermute(lax.slice_in_dim(block, 0, width, axis=dim), axis, backward)
        block = jnp.concatenate([low, block, high], axis=dim)
    return block


def gather_weights(qkv_weight, out_weight):
    qkv_rows, qkv_cols = qkv_weight.shape
    out_rows, out_cols = out_weight.shape
    out_wide = out_weight.reshape(qkv_rows, out_rows * out_cols // qkv_rows)
    both = lax.all_gather(
        jnp.concatenate([qkv_weight, out_wide], axis=1), "tensor", axis=0, tiled=True
    )
    full_qkv = both[:, :qkv_cols]
    out_pairs = both[:, qkv_cols:]
    return (full_qkv, out_pairs)


def spread(cols, side):
    rows = cols.shape[0]
    none = jnp.zeros_like(cols)
    pair = (cols, none) if side == 0 else (none, cols)
    return jnp.stack(pair, axis=-1).reshape(rows, 2 * cols.shape[1])


def times_out(attended, out_pairs):
    halves = [
        jnp.dot(spread(attended, side), out_pairs, preferred_element_type=jnp.float32)
        for side in range(2)
    ]
    return jnp.concatenate(halves, axis=1)


def times_out_t(grad_rows, out_pairs):
    half = out_pairs.shape[1]
    rows = grad_rows.shape[0]
    parts = [
        lax.dot_general(
            grad_rows[:, side * half : (side + 1) * half],
            out_pairs,
            (((1,), (1,)), ((), ())),
            preferred_element_type=jnp.float32,
        )
        for side in range(2)
    ]
    even = lax.broadcasted_iota(jnp.int32, parts[0].shape, 1) % 2 == 0
    return jnp.where(even, parts[0], parts[1]).reshape(rows, -1, 2).sum(axis=2)


def normalize(rows_in, norm_gain):
    values = rows_in.astype(jnp.float32)
    center = values - jnp.mean(values, axis=-1, keepdims=True)
    inv_dev = lax.rsqrt(jnp.mean(center * center, axis=-1, keepdims=True) + 1e-06)
    unit_rows = center * inv_dev
    return (values, unit_rows, inv_dev, (unit_rows * norm_gain).astype(jnp.bfloat16))


def head_blocks(rows_in, count):
    tiled = jnp.tile(rows_in, (HEADS, 1))
    row_head = lax.broadcasted_iota(jnp.int32, tiled.shape, 0) // count
    col_head = lax.broadcasted_iota(jnp.int32, tiled.shape, 1) // HD
    return jnp.where(row_head == col_head, tiled, jnp.zeros_like(tiled))


def own_heads(stacked, count):
    row_head = lax.broadcasted_iota(jnp.int32, stacked.shape, 0) // count
    col_head = lax.broadcasted_iota(jnp.int32, stacked.shape, 1) // HD
    kept = jnp.where(row_head == col_head, stacked, jnp.zeros_like(stacked))
    return kept.reshape(HEADS, count, stacked.shape[1]).sum(axis=0)


def rows_dot(a, b):
    return lax.dot_general(a, b, (((1,), (1,)), ((), ())), preferred_element_type=jnp.float32)


def cols_dot(a, b):
    return lax.dot_general(a, b, (((0,), (0,)), ((), ())), preferred_element_type=jnp.float32)


def attend(queries, keyval, seg_query, seg_key):
    all_heads = HEADS * HD
    score_scale = HD ** (-0.5)
    count = queries.shape[0]
    query_blocks = head_blocks(queries, count)
    scores = rows_dot(query_blocks, keyval[:, :all_heads]) * score_scale
    same_chart = jnp.tile(seg_query[:, None] == seg_key[None, :], (HEADS, 1))
    scores = jnp.where(same_chart, scores, -jnp.inf)
    row_max = jnp.max(scores, axis=1, keepdims=True)
    exp_scores = jnp.exp(scores - row_max)
    row_sum = jnp.sum(exp_scores, axis=1, keepdims=True)
    attn_probs = exp_scores / row_sum
    prob_low = attn_probs.astype(jnp.bfloat16)
    mixed = jnp.dot(prob_low, keyval[:, all_heads:], preferred_element_type=jnp.float32)
    attended = own_heads(mixed, count)
    return (attn_probs, prob_low, attended.astype(jnp.bfloat16), query_blocks)


def local(patch_rows, send_rows, take_rows, segments, norm_gain, qkv_weight, out_weight, grad_out):
    groups = lax.axis_size("dp")
    src_count = patch_rows.shape[1]
    features = patch_rows.shape[2]
    slot_count = send_rows.shape[3]
    own_rows = take_rows.shape[1]
    all_heads = HEADS * HD
    score_scale = HD ** (-0.5)
    patches = patch_rows[0]
    send_flat = send_rows.reshape(groups * slot_count)
    outgoing = jnp.take(patches, send_flat, axis=0, mode="fill", fill_value=0).reshape(
        groups, slot_count, features
    )
    incoming = lax.all_to_all(outgoing, "dp", split_axis=0, concat_axis=0, tiled=True).reshape(
        groups * slot_count, features
    )
    pick_rows = take_rows[0]
    slot_total = groups * slot_count
    row_slot = (
        jnp.full((src_count + 1,), slot_total, jnp.int32)
        .at[send_flat]
        .set(jnp.arange(slot_total, dtype=jnp.int32))[:src_count]
    )
    packed = jnp.take(incoming, pick_rows, axis=0)
    full_qkv, full_out = gather_weights(qkv_weight, out_weight)
    values, unit_rows, inv_dev, normed = normalize(packed, norm_gain)
    projected = jnp.dot(normed, full_qkv, preferred_element_type=jnp.float32).astype(jnp.bfloat16)
    queries = projected[:, :all_heads]
    keyval = projected[:, all_heads:]
    seg_plus = segments[0] + 1
    wide_kv, wide_seg = (
        extended(keyval, (("tensor", 0),), MOST),
        extended(seg_plus, (("tensor", 0),), MOST),
    )
    attn_probs, prob_low, attended, query_blocks = attend(queries, wide_kv, seg_plus, wide_seg)
    layer_out = (values + times_out(attended, full_out)).astype(jnp.bfloat16)
    grad_rows = grad_out[0]
    grad_att = times_out_t(grad_rows, full_out).astype(jnp.bfloat16)
    grad_blocks = head_blocks(grad_att, own_rows)
    dprobs = rows_dot(grad_blocks, wide_kv[:, all_heads:])
    row_inner = jnp.sum(attn_probs * dprobs, axis=1, keepdims=True)
    dscore = (attn_probs * (dprobs - row_inner) * score_scale).astype(jnp.bfloat16)
    window_rows = wide_kv.shape[0]
    score_rows = dscore.reshape(HEADS, own_rows, window_rows).transpose(1, 0, 2)
    grad_query = jnp.dot(
        score_rows.reshape(own_rows, HEADS * window_rows),
        head_blocks(wide_kv[:, :all_heads], window_rows),
        preferred_element_type=jnp.float32,
    )
    grad_key = cols_dot(dscore, query_blocks)
    grad_value = cols_dot(prob_low, grad_blocks)
    grad_window = jnp.concatenate([grad_key, grad_value], axis=1)
    center = grad_window[MOST : MOST + own_rows]
    blocks = lax.axis_size("tensor")
    ahead = [(i, i + 1) for i in range(blocks - 1)]
    behind = [(target, source) for source, target in ahead]
    high_rim, low_rim = lax.optimization_barrier(
        (grad_window[MOST + own_rows :], grad_window[:MOST])
    )
    from_prev = lax.ppermute(high_rim, "tensor", ahead)
    from_next = lax.ppermute(low_rim, "tensor", behind)
    center = center.at[:MOST].add(from_prev)
    center = center.at[own_rows - MOST :].add(from_next)
    grad_proj = jnp.concatenate([grad_query, center], axis=1).astype(jnp.bfloat16)
    grad_normed = lax.dot_general(
        grad_proj, full_qkv, (((1,), (1,)), ((), ())), preferred_element_type=jnp.float32
    )
    scaled = grad_normed * norm_gain
    grad_unit = (
        scaled
        - jnp.mean(scaled, axis=-1, keepdims=True)
        - unit_rows * jnp.mean(scaled * unit_rows, axis=-1, keepdims=True)
    )
    grad_packed = (grad_rows.astype(jnp.float32) + inv_dev * grad_unit).astype(jnp.bfloat16)
    back_slots = (
        jnp.zeros((groups * slot_count, features), jnp.bfloat16).at[pick_rows].set(grad_packed)
    )
    back_slots = back_slots.reshape(groups, slot_count, features)
    returned = lax.all_to_all(back_slots, "dp", split_axis=0, concat_axis=0, tiled=True).reshape(
        groups * slot_count, features
    )
    patch_grad = jnp.take(returned, row_slot, axis=0, mode="fill", fill_value=0)
    return (layer_out[None], patch_grad[None])


def solution(mesh):
    return jax.shard_map(
        local,
        mesh=mesh,
        in_specs=(
            P("dp", "tensor", None),
            P("dp", "tensor", None, None),
            P("dp", "tensor"),
            P("dp", "tensor"),
            P(),
            P("tensor", None),
            P("tensor", None),
            P("dp", "tensor", None),
        ),
        out_specs=(P("dp", "tensor", None), P("dp", "tensor", None)),
        check_vma=False,
    )
```

profile of v0, /device:TPU:66, one launch (start us, length us, event | category | flops | bytes accessed | tf_op | source)
XLA Modules:
  0.0 185.1 jit_solution(1266978088564810541)
XLA Ops:
  7.2 1.1 reshape.392
  8.3 2.0 %pad_maximum_fusion.1 = bf16[112,3584]{1,0:T(8,128)(2,1)} fusion(bf16[112,896]{1,0:T(8,128)(2,1)S(1)} %reshape.392, bf16[112,2688]{1,0:T(8,128)(2,1)} %param.19), kind=kLoop, calls=%fused_computation.67 | loop fusion | flops 1605632 | bytes 1605632 | tf_op jit(solution)/shard_map/concatenate | solution.py:29
  10.6 1.1 gather_fusion.1
  11.9 1.2 reshape.390
  13.1 10.2 %all-to-all-start = ((bf16[32,6,1792]{2,1,0:T(8,128)(2,1)}), bf16[32,6,1792]{2,1,0:T(8,128)(2,1)S(1)}, u32[]{:S(2)}, u32[]{:S(2)}) async-start(bf16[32,6,1792]{2,1,0:T(8,128)(2,1)} %reshape.390), calls=%async_computation | async-start | bytes 1835008 | tf_op jit(solution)/shard_map/all_to_all | solution.py:128
  23.4 1.9 %collective-permute-start = (s32[96]{0:T(128)S(1)}, s32[96]{0:T(128)S(1)}, u32[]{:S(2)}, u32[]{:S(2)}) collective-permute-start(s32[96]{0:T(128)S(1)} %get-tuple-element.41), channel_id=1, source_target_pairs={{0,1},{1,2},{2,3},{3,4},{4,5},{5,6},{6,7},{7,8},{8,9},{9,10},{10,1... | collective-permute-start | bytes 1160 | tf_op jit(solution)/shard_map/ppermute | solution.py:16
  25.3 3.6 %collective-permute-start.1 = (s32[96]{0:T(128)S(1)}, s32[96]{0:T(128)S(1)}, u32[]{:S(2)}, u32[]{:S(2)}) collective-permute-start(s32[96]{0:T(128)S(1)} %get-tuple-element.42), channel_id=1, source_target_pairs={{1,0},{2,1},{3,2},{4,3},{5,4},{6,5},{7,6},{8,7},{9,8},{10,9},{11,1... | collective-permute-start | bytes 1160 | tf_op jit(solution)/shard_map/ppermute | solution.py:19
  29.1 1.2 scatter_custom_fusion.1
  35.7 0.8 copy.27
  36.5 0.8 copy.28
  37.3 0.8 copy.26
  38.1 0.7 broadcast_compare_fusion
  38.8 9.7 %all-to-all-done = bf16[32,6,1792]{2,1,0:T(8,128)(2,1)S(1)} async-done(((bf16[32,6,1792]{2,1,0:T(8,128)(2,1)}), bf16[32,6,1792]{2,1,0:T(8,128)(2,1)S(1)}, u32[]{:S(2)}, u32[]{:S(2)}) %all-to-all-start) | async-done | bytes 688160 | tf_op jit(solution)/shard_map/all_to_all | solution.py:128
  48.8 0.9 gather_fusion
  50.3 42.0 %all-gather.2.cloned.1.call-done = bf16[1792,3584]{1,0:T(8,128)(2,1)} async-done(((bf16[112,3584]{1,0:T(8,128)(2,1)}), bf16[1792,3584]{1,0:T(8,128)(2,1)}) %all-gather.2.cloned.1.call-update) | async-done | bytes 12845072 | tf_op jit(solution)/shard_map/all_gather | solution.py:28
  92.3 5.5 %fusion.9 = bf16[128,2688]{1,0:T(8,128)(2,1)S(1)} fusion(bf16[1792,3584]{1,0:T(8,128)(2,1)} %all-gather.2.cloned.1.call-done, f32[1792]{0:T(1024)S(1)} %copy-done.27, f32[128]{0:T(128)S(1)} %add_rsqrt_fusion, f32[128]{0:T(128)S(1)} %broadcast_multiply_fusion.2, bf16[128,1792]{1,0:T(8,128)(2,1)S(1)} %gather_fusion, pred[128]{0:T(512)(128)(4,1)S(1)} %compare_and_fusion.2), kind=kOutput, calls=%fused_computation.15 | convolution fusion | flops 1234845696 | bytes 10788992 | tf_op jit(solution)/shard_map/dot_general | solution.py:141
  97.9 0.8 fusion.107
  98.7 2.3 %collective-permute-start.2 = (bf16[96,1792]{1,0:T(8,128)(2,1)}, bf16[96,1792]{1,0:T(8,128)(2,1)S(1)}, u32[]{:S(2)}, u32[]{:S(2)}) collective-permute-start(bf16[96,1792]{1,0:T(8,128)(2,1)} %get-tuple-element.35), channel_id=1, source_target_pairs={{0,1},{1,2},{2,3},{3,4},{4,5},{5,6},{6,7},{7,8},{8,9},{9,10},{10,1... | collective-permute-start | bytes 1032200 | tf_op jit(solution)/shard_map/ppermute | solution.py:16
  101.0 4.5 %collective-permute-start.3 = (bf16[96,1792]{1,0:T(8,128)(2,1)S(1)}, bf16[96,1792]{1,0:T(8,128)(2,1)S(1)}, u32[]{:S(2)}, u32[]{:S(2)}) collective-permute-start(bf16[96,1792]{1,0:T(8,128)(2,1)S(1)} %get-tuple-element.36), channel_id=1, source_target_pairs={{1,0},{2,1},{3,2},{4,3},{5,4},{6,5},{7,6},{8,7},{9,8},{10,9},{11,1... | collective-permute-start | bytes 1032200 | tf_op jit(solution)/shard_map/ppermute | solution.py:19
  105.6 1.0 convolution_bitcast_fusion.1
  106.6 1.0 fusion.12
  107.7 1.2 reduce_sum.76
  109.1 1.8 fusion.18
  111.0 0.6 copy-done.7
  111.8 1.0 fusion.109
  113.0 0.9 multiply_reduce_fusion
  113.9 0.9 fusion.79
  115.1 0.8 fusion.110
  116.3 2.1 %collective-permute-start.4 = (f32[96,1792]{1,0:T(8,128)S(1)}, f32[96,1792]{1,0:T(8,128)S(1)}, u32[]{:S(2)}, u32[]{:S(2)}) collective-permute-start(f32[96,1792]{1,0:T(8,128)S(1)} %get-tuple-element.29), channel_id=1, source_target_pairs={{0,1},{1,2},{2,3},{3,4},{4,5},{5,6},{6,7},{7,8},{8,9},{9,10},{10,1... | collective-permute-start | bytes 2064392 | tf_op jit(solution)/shard_map/ppermute | solution.py:174
  118.3 3.9 %collective-permute-start.5 = (f32[96,1792]{1,0:T(8,128)S(1)}, f32[96,1792]{1,0:T(8,128)S(1)}, u32[]{:S(2)}, u32[]{:S(2)}) collective-permute-start(f32[96,1792]{1,0:T(8,128)S(1)} %get-tuple-element.30), channel_id=1, source_target_pairs={{1,0},{2,1},{3,2},{4,3},{5,4},{6,5},{7,6},{8,7},{9,8},{10,9},{11,1... | collective-permute-start | bytes 2064392 | tf_op jit(solution)/shard_map/ppermute | solution.py:175
  122.3 1.8 fusion.37
  124.2 4.5 %collective-permute-done.4 = f32[96,1792]{1,0:T(8,128)S(1)} collective-permute-done((f32[96,1792]{1,0:T(8,128)S(1)}, f32[96,1792]{1,0:T(8,128)S(1)}, u32[]{:S(2)}, u32[]{:S(2)}) %collective-permute-start.4) | collective-permute-done | bytes 688160 | tf_op jit(solution)/shard_map/ppermute | solution.py:174
  128.8 1.6 collective-permute-done.5
  130.7 3.7 %fusion.106 = (f32[128]{0:T(128)S(1)}, f32[128]{0:T(128)S(1)}, f32[128,1792]{1,0:T(8,128)}) fusion(f32[128]{0:T(128)S(1)} %copy-done.26, f32[128]{0:T(128)S(1)} %copy-done.20, bf16[128,1792]{1,0:T(8,128)(2,1)S(1)} %gather_fusion, pred[128]{0:T(512)(128)(4,1)S(1)} %copy-done.16, f32[1792]{0:T(1024)S(1)} %copy-done.28, bf16[1792,3584]{1,0:T(8,128)(2,1)S(1)} %bitcast.76, ...), kind=kOutput, calls=%fused_computation.154 | convolution fusion | flops 1236336384 | bytes 11708928 | tf_op jit(solution)/shard_map/dot_general | solution.py:179
  134.4 2.6 %scatter_custom_fusion = bf16[192,1792]{1,0:T(8,128)(2,1)S(1)} fusion(s32[128]{0:T(128)} %copy-done.24, f32[128,1792]{1,0:T(8,128)} %get-tuple-element.49, f32[128]{0:T(128)S(1)} %broadcast_multiply_fusion, f32[128]{0:T(128)S(1)} %broadcast_multiply_fusion.1, f32[128]{0:T(128)S(1)} %copy-done.26, f32[128]{0:T(128)S(1)} %copy-done.20, ...), kind=kCustom, calls=%fused_computation.84 | custom fusion | flops 2523136 | bytes 2525824 | tf_op jit(solution)/shard_map/scatter | solution.py:190
  137.1 1.2 reshape.398
  138.2 9.9 %all-to-all-start.1 = ((bf16[32,6,1792]{2,1,0:T(8,128)(2,1)}), bf16[32,6,1792]{2,1,0:T(8,128)(2,1)}, u32[]{:S(2)}, u32[]{:S(2)}) async-start(bf16[32,6,1792]{2,1,0:T(8,128)(2,1)} %reshape.398), calls=%async_computation.1 | async-start | bytes 1835008 | tf_op jit(solution)/shard_map/all_to_all | solution.py:193
  148.2 3.8 %fusion.19 = f32[1024,896]{1,0:T(8,128)} fusion(s32[896]{0:T(1024)S(1)} %copy-done.9, s32[896]{0:T(1024)S(1)} %copy-done.10, s32[1024]{0:T(1024)S(1)} %copy-done.11, s32[1024]{0:T(1024)S(1)} %copy-done.12, pred[1024]{0:T(1024)(128)(4,1)S(1)} %copy-done.22, pred[896]{0:T(1024)(128)(4,1)S(1)} %copy-done.21, bf16[320,1792]{1,0:T(8,128)(2,1)} %copy-done.3, ...), kind=kOutput, calls=%fused_computation.29 | convolution fusion | flops 591855616 | bytes 5579648 | tf_op jit(solution)/shard_map/dot_general | solution.py:110
  152.0 2.2 %reduce_sum.75 = bf16[128,896]{1,0:T(8,128)(2,1)S(1)} reduce(f32[8,128,896]{2,1,0:T(8,128)} %bitcast.74, f32[]{:T(128)} %constant.161.clone.1), dimensions={0}, to_apply=%region_4.6 | reduce | flops 802816 | bytes 3899396 | tf_op jit(solution)/shard_map/reduce_sum | solution.py:86
  154.2 0.8 copy.29
  155.0 1.1 fusion.108
  156.2 2.6 %fusion.28 = f32[1,128,896]{2,1,0:T(8,128)S(1)} fusion(bf16[128,1792]{0,1:T(8,128)(2,1)S(1)} %bitcast.79, bf16[1792,3584]{1,0:T(8,128)(2,1)} %all-gather.2.cloned.1.call-done), kind=kOutput, calls=%fused_computation.42 | convolution fusion | flops 411041792 | bytes 4128768 | tf_op jit(solution)/shard_map/dot_general | solution.py:45
  158.8 2.6 %fusion.31 = f32[1,128,896]{2,1,0:T(8,128)S(1)} fusion(bf16[128,1792]{0,1:T(8,128)(2,1)S(1)} %bitcast.78, bf16[1792,3584]{1,0:T(8,128)(2,1)} %all-gather.2.cloned.1.call-done), kind=kOutput, calls=%fused_computation.43 | convolution fusion | flops 411041792 | bytes 4128768 | tf_op jit(solution)/shard_map/dot_general | solution.py:45
  161.4 1.0 fusion.55
  162.3 12.3 %all-to-all-done.1 = bf16[32,6,1792]{2,1,0:T(8,128)(2,1)} async-done(((bf16[32,6,1792]{2,1,0:T(8,128)(2,1)}), bf16[32,6,1792]{2,1,0:T(8,128)(2,1)}, u32[]{:S(2)}, u32[]{:S(2)}) %all-to-all-start.1) | async-done | bytes 688160 | tf_op jit(solution)/shard_map/all_to_all | solution.py:193
  174.6 1.4 reshape.399
  176.0 1.3 gather_fusion.2
  177.3 1.0 select_bitcast_fusion
  (127 shorter events, 8.4 us)
Async XLA Ops:
  7.2 3.4 %copy-start = (bf16[1,192,1792]{2,1,0:T(8,128)(2,1)S(1)}, bf16[1,192,1792]{2,1,0:T(8,128)(2,1)}, u32[]{:S(2)}) copy-start(bf16[1,192,1792]{2,1,0:T(8,128)(2,1)} %param.14) | copy-start | bytes 2064388
  7.2 3.2 %copy-start.17 = (s32[1,1,32,6]{2,1,3,0:T(1,128)S(1)}, s32[1,1,32,6]{2,1,3,0:T(1,128)}, u32[]{:S(2)}) copy-start(s32[1,1,32,6]{2,1,3,0:T(1,128)} %param.15) | copy-start | bytes 2308
  7.2 85.1 %all-gather.2.cloned.1.call-start = ((), (), s32[]{:S(2)}) async-start(), calls=%async_computation.2 | async-start | bytes 13647872 | tf_op jit(solution)/shard_map/all_gather | solution.py:28
  11.9 11.4 %copy-start.29 = (s32[1,128]{1,0:T(1,128)S(1)}, s32[1,128]{1,0:T(1,128)}, u32[]{:S(2)}) copy-start(s32[1,128]{1,0:T(1,128)} %param.17) | copy-start | bytes 1540
  11.9 19.0 %copy-start.30 = (s32[1,128]{1,0:T(1,128)S(1)}, s32[1,128]{1,0:T(1,128)}, u32[]{:S(2)}) copy-start(s32[1,128]{1,0:T(1,128)} %param.16) | copy-start | bytes 1540
  13.1 35.5 %all-to-all-start = ((bf16[32,6,1792]{2,1,0:T(8,128)(2,1)}), bf16[32,6,1792]{2,1,0:T(8,128)(2,1)S(1)}, u32[]{:S(2)}, u32[]{:S(2)}) async-start(bf16[32,6,1792]{2,1,0:T(8,128)(2,1)} %reshape.390), calls=%async_computation | async-start | bytes 1835008 | tf_op jit(solution)/shard_map/all_to_all | solution.py:128
  23.4 14.6 %collective-permute-start = (s32[96]{0:T(128)S(1)}, s32[96]{0:T(128)S(1)}, u32[]{:S(2)}, u32[]{:S(2)}) collective-permute-start(s32[96]{0:T(128)S(1)} %get-tuple-element.41), channel_id=1, source_target_pairs={{0,1},{1,2},{2,3},{3,4},{4,5},{5,6},{6,7},{7,8},{8,9},{9,10},{10,1... | collective-permute-start | bytes 1160 | tf_op jit(solution)/shard_map/ppermute | solution.py:16
  25.3 12.7 %collective-permute-start.1 = (s32[96]{0:T(128)S(1)}, s32[96]{0:T(128)S(1)}, u32[]{:S(2)}, u32[]{:S(2)}) collective-permute-start(s32[96]{0:T(128)S(1)} %get-tuple-element.42), channel_id=1, source_target_pairs={{1,0},{2,1},{3,2},{4,3},{5,4},{6,5},{7,6},{8,7},{9,8},{10,9},{11,1... | collective-permute-start | bytes 1160 | tf_op jit(solution)/shard_map/ppermute | solution.py:19
  30.9 0.6 copy-start.24
  34.6 57.7 %copy-start.15 = (pred[128]{0:T(512)(128)(4,1)}, pred[128]{0:T(512)(128)(4,1)S(1)}, u32[]{:S(2)}) copy-start(pred[128]{0:T(512)(128)(4,1)S(1)} %compare_and_fusion.2) | copy-start | bytes 388
  48.8 43.5 %copy-start.27 = (f32[1792]{0:T(1024)S(1)}, f32[1792]{0:T(1024)}, u32[]{:S(2)}) copy-start(f32[1792]{0:T(1024)} %param.18) | copy-start | bytes 21508
  50.0 47.9 %copy-start.19 = (f32[128]{0:T(128)}, f32[128]{0:T(128)S(1)}, u32[]{:S(2)}) copy-start(f32[128]{0:T(128)S(1)} %broadcast_multiply_fusion.2) | copy-start | bytes 1540
  50.3 47.6 %copy-start.25 = (f32[128]{0:T(128)}, f32[128]{0:T(128)S(1)}, u32[]{:S(2)}) copy-start(f32[128]{0:T(128)S(1)} %add_rsqrt_fusion) | copy-start | bytes 1540
  92.3 13.2 %copy-start.1 = (bf16[1792,3584]{1,0:T(8,128)(2,1)S(1)}, bf16[1792,3584]{1,0:T(8,128)(2,1)}, u32[]{:S(2)}) copy-start(bf16[1792,3584]{1,0:T(8,128)(2,1)} %all-gather.2.cloned.1.call-done) | copy-start | bytes 38535172
  97.9 8.7 %copy-start.2 = (bf16[128,2688]{1,0:T(8,128)(2,1)}, bf16[128,2688]{1,0:T(8,128)(2,1)S(1)}, u32[]{:S(2)}) copy-start(bf16[128,2688]{1,0:T(8,128)(2,1)S(1)} %fusion.9) | copy-start | bytes 2064388
  97.9 7.6 %copy-start.4 = (bf16[1,128,1792]{2,1,0:T(8,128)(2,1)S(1)}, bf16[1,128,1792]{2,1,0:T(8,128)(2,1)}, u32[]{:S(2)}) copy-start(bf16[1,128,1792]{2,1,0:T(8,128)(2,1)} %param.21) | copy-start | bytes 1376260
  98.7 12.2 %collective-permute-start.2 = (bf16[96,1792]{1,0:T(8,128)(2,1)}, bf16[96,1792]{1,0:T(8,128)(2,1)S(1)}, u32[]{:S(2)}, u32[]{:S(2)}) collective-permute-start(bf16[96,1792]{1,0:T(8,128)(2,1)} %get-tuple-element.35), channel_id=1, source_target_pairs={{0,1},{1,2},{2,3},{3,4},{4,5},{5,6},{6,7},{7,8},{8,9},{9,10},{10,1... | collective-permute-start | bytes 1032200 | tf_op jit(solution)/shard_map/ppermute | solution.py:16
  101.0 9.9 %collective-permute-start.3 = (bf16[96,1792]{1,0:T(8,128)(2,1)S(1)}, bf16[96,1792]{1,0:T(8,128)(2,1)S(1)}, u32[]{:S(2)}, u32[]{:S(2)}) collective-permute-start(bf16[96,1792]{1,0:T(8,128)(2,1)S(1)} %get-tuple-element.36), channel_id=1, source_target_pairs={{1,0},{2,1},{3,2},{4,3},{5,4},{6,5},{7,6},{8,7},{9,8},{10,9},{11,1... | collective-permute-start | bytes 1032200 | tf_op jit(solution)/shard_map/ppermute | solution.py:19
  105.5 1.1 copy-start.13
  105.5 1.1 copy-start.14
  105.6 1.1 copy-start.18
  106.6 2.4 %slice-start.5 = ((bf16[128,2688]{1,0:T(8,128)(2,1)}), bf16[128,896]{1,0:T(8,128)(2,1)S(1)}, s32[]{:S(2)}) async-start(bf16[128,2688]{1,0:T(8,128)(2,1)} %copy-done.2), calls=%async_computation.8 | async-start | bytes 458752 | tf_op jit(solution)/shard_map/slice | solution.py:142
  109.1 1.8 slice-start.4
  110.9 0.8 copy-start.7
  111.0 2.0 %copy-start.3 = (bf16[320,1792]{1,0:T(8,128)(2,1)}, bf16[320,1792]{1,0:T(8,128)(2,1)S(1)}, u32[]{:S(2)}) copy-start(bf16[320,1792]{1,0:T(8,128)(2,1)S(1)} %pad_maximum_fusion) | copy-start | bytes 3440644
  116.1 6.1 %slice-start.6 = ((bf16[320,1792]{1,0:T(8,128)(2,1)}), bf16[320,896]{1,0:T(8,128)(2,1)S(1)}, s32[]{:S(2)}) async-start(bf16[320,1792]{1,0:T(8,128)(2,1)} %copy-done.3), calls=%async_computation.9 | async-start | bytes 1146880 | tf_op jit(solution)/shard_map/slice | solution.py:102
  116.1 6.1 %copy-start.5 = (s32[8,320]{0,1:T(8,128)S(1)}, s32[8,320]{0,1:T(8,128)}, u32[]{:S(2)}) copy-start(s32[8,320]{0,1:T(8,128)} %copy.27) | copy-start | bytes 30724
  116.1 6.1 %copy-start.6 = (s32[8,320]{0,1:T(8,128)S(1)}, s32[8,320]{0,1:T(8,128)}, u32[]{:S(2)}) copy-start(s32[8,320]{0,1:T(8,128)} %copy.28) | copy-start | bytes 30724
  116.1 6.1 %copy-start.8 = (pred[8,320]{0,1:T(8,128)(4,1)S(1)}, pred[8,320]{0,1:T(8,128)(4,1)}, u32[]{:S(2)}) copy-start(pred[8,320]{0,1:T(8,128)(4,1)} %copy.26) | copy-start | bytes 7684
  116.2 6.1 %copy-start.9 = (s32[896]{0:T(1024)S(1)}, s32[896]{0:T(1024)}, u32[]{:S(2)}) copy-start(s32[896]{0:T(1024)} %get-tuple-element.52) | copy-start | bytes 10756
  116.2 6.1 %copy-start.10 = (s32[896]{0:T(1024)S(1)}, s32[896]{0:T(1024)}, u32[]{:S(2)}) copy-start(s32[896]{0:T(1024)} %get-tuple-element.53) | copy-start | bytes 10756
  116.2 6.1 %copy-start.21 = (pred[896]{0:T(1024)(128)(4,1)S(1)}, pred[896]{0:T(1024)(128)(4,1)}, u32[]{:S(2)}) copy-start(pred[896]{0:T(1024)(128)(4,1)} %fusion.94) | copy-start | bytes 2692
  116.3 12.4 %collective-permute-start.4 = (f32[96,1792]{1,0:T(8,128)S(1)}, f32[96,1792]{1,0:T(8,128)S(1)}, u32[]{:S(2)}, u32[]{:S(2)}) collective-permute-start(f32[96,1792]{1,0:T(8,128)S(1)} %get-tuple-element.29), channel_id=1, source_target_pairs={{0,1},{1,2},{2,3},{3,4},{4,5},{5,6},{6,7},{7,8},{8,9},{9,10},{10,1... | collective-permute-start | bytes 2064392 | tf_op jit(solution)/shard_map/ppermute | solution.py:174
  118.3 12.1 %collective-permute-start.5 = (f32[96,1792]{1,0:T(8,128)S(1)}, f32[96,1792]{1,0:T(8,128)S(1)}, u32[]{:S(2)}, u32[]{:S(2)}) collective-permute-start(f32[96,1792]{1,0:T(8,128)S(1)} %get-tuple-element.30), channel_id=1, source_target_pairs={{1,0},{2,1},{3,2},{4,3},{5,4},{6,5},{7,6},{8,7},{9,8},{10,9},{11,1... | collective-permute-start | bytes 2064392 | tf_op jit(solution)/shard_map/ppermute | solution.py:175
  122.3 8.3 %slice-start = ((s8[12845056]{0:T(1024)(128)(4,1)}), s8[4194304]{0:T(1024)(128)(4,1)S(1)}, s32[]{:S(2)}) async-start(s8[12845056]{0:T(1024)(128)(4,1)} %bitcast.75), calls=%async_computation.3 | async-start | bytes 8388608
  122.3 8.3 %slice-start.1 = ((s8[12845056]{0:T(1024)(128)(4,1)}), s8[4194304]{0:T(1024)(128)(4,1)S(1)}, s32[]{:S(2)}) async-start(s8[12845056]{0:T(1024)(128)(4,1)} %bitcast.75), calls=%async_computation.4 | async-start | bytes 8388608
  122.3 8.3 %slice-start.2 = ((s8[12845056]{0:T(1024)(128)(4,1)}), s8[4194304]{0:T(1024)(128)(4,1)S(1)}, s32[]{:S(2)}) async-start(s8[12845056]{0:T(1024)(128)(4,1)} %bitcast.75), calls=%async_computation.5 | async-start | bytes 8388608
  124.1 6.5 %slice-start.3 = ((s8[12845056]{0:T(1024)(128)(4,1)}), s8[262144]{0:T(1024)(128)(4,1)S(1)}, s32[]{:S(2)}) async-start(s8[12845056]{0:T(1024)(128)(4,1)} %bitcast.75), calls=%async_computation.6 | async-start | bytes 524288
  128.7 1.9 %copy-start.16 = (pred[128]{0:T(512)(128)(4,1)S(1)}, pred[128]{0:T(512)(128)(4,1)}, u32[]{:S(2)}) copy-start(pred[128]{0:T(512)(128)(4,1)} %copy-done.15) | copy-start | bytes 388
  128.8 1.9 %copy-start.20 = (f32[128]{0:T(128)S(1)}, f32[128]{0:T(128)}, u32[]{:S(2)}) copy-start(f32[128]{0:T(128)} %copy-done.19) | copy-start | bytes 1540
  128.8 1.9 %copy-start.26 = (f32[128]{0:T(128)S(1)}, f32[128]{0:T(128)}, u32[]{:S(2)}) copy-start(f32[128]{0:T(128)} %copy-done.25) | copy-start | bytes 1540
  128.8 1.9 %copy-start.28 = (f32[1792]{0:T(1024)S(1)}, f32[1792]{0:T(1024)}, u32[]{:S(2)}) copy-start(f32[1792]{0:T(1024)} %param.18) | copy-start | bytes 21508
  137.1 11.1 %copy-start.11 = (s32[1024]{0:T(1024)S(1)}, s32[1024]{0:T(1024)}, u32[]{:S(2)}) copy-start(s32[1024]{0:T(1024)} %get-tuple-element.54) | copy-start | bytes 12292
  137.1 11.1 %copy-start.12 = (s32[1024]{0:T(1024)S(1)}, s32[1024]{0:T(1024)}, u32[]{:S(2)}) copy-start(s32[1024]{0:T(1024)} %get-tuple-element.55) | copy-start | bytes 12292
  137.1 11.1 %copy-start.22 = (pred[1024]{0:T(1024)(128)(4,1)S(1)}, pred[1024]{0:T(1024)(128)(4,1)}, u32[]{:S(2)}) copy-start(pred[1024]{0:T(1024)(128)(4,1)} %fusion.95) | copy-start | bytes 3076
  138.2 36.4 %all-to-all-start.1 = ((bf16[32,6,1792]{2,1,0:T(8,128)(2,1)}), bf16[32,6,1792]{2,1,0:T(8,128)(2,1)}, u32[]{:S(2)}, u32[]{:S(2)}) async-start(bf16[32,6,1792]{2,1,0:T(8,128)(2,1)} %reshape.398), calls=%async_computation.1 | async-start | bytes 1835008 | tf_op jit(solution)/shard_map/all_to_all | solution.py:193
  176.0 1.3 copy-start.23
Sparse Core Ops, SparseCore 0:
  10.5 81.8 all-gather.1
where the time goes:
time: 186 us; the launch traced here: 185 us
  waiting for transfers between devices  70.2 us (38%)
  starting transfers between devices  38.5 us (21%)
  matrix products  25.7 us (14%)
  other arithmetic  19.1 us (10%)
  local copies, waits for them, and re-layouts  16.7 us (9%)
  between operations  15 us (8%)
    all_gather x1, waiting for transfers between devices, gather_weights(): lax.all_gather(jnp.concatenate([qkv_weight, out_wide], axis=1), 'tensor',...  42 us
    all_to_all x1, waiting for transfers between devices, local(): lax.all_to_all(back_slots, 'dp', split_axis=0, concat_axis=0, tiled=True)  12.3 us
    all_to_all x1, starting transfers between devices, local(): lax.all_to_all(outgoing, 'dp', split_axis=0, concat_axis=0, tiled=True)  10.2 us
    all_to_all x1, starting transfers between devices, local(): lax.all_to_all(back_slots, 'dp', split_axis=0, concat_axis=0, tiled=True)  9.91 us
    all_to_all x1, waiting for transfers between devices, local(): lax.all_to_all(outgoing, 'dp', split_axis=0, concat_axis=0, tiled=True)  9.75 us
    ppermute x2, starting transfers between devices, extended(): lax.ppermute(lax.slice_in_dim(block, 0, width, axis=dim), axis, backward)  8.16 us
    dot_general x1, matrix products, local(): jnp.dot(normed, full_qkv, preferred_element_type=jnp.float32)  5.54 us
    dot_general x2, matrix products, times_out(): jnp.dot(spread(attended, side), out_pairs, preferred_element_type=jnp.flo...  5.18 us
  transfers between devices with their start and end apart: 9, of which 5 were waited for; matrix products, arithmetic and copies ran while one was open for 19% of the time, Pallas kernels for 0%

commit v1 on v0

--- a/solution.py
+++ b/solution.py
@@ -25,8 +25,14 @@
     qkv_rows, qkv_cols = qkv_weight.shape
     out_rows, out_cols = out_weight.shape
     out_wide = out_weight.reshape(qkv_rows, out_rows * out_cols // qkv_rows)
-    both = lax.all_gather(
-        jnp.concatenate([qkv_weight, out_wide], axis=1), "tensor", axis=0, tiled=True
+    both = jnp.concatenate(
+        lax.all_to_all(
+            jnp.stack([jnp.concatenate([qkv_weight, out_wide], axis=1)] * lax.axis_size("tensor")),
+            "tensor",
+            0,
+            0,
+        ),
+        axis=0,
     )
     full_qkv = both[:, :qkv_cols]
     out_pairs = both[:, qkv_cols:]

time: 186 us -> 421 us (2.26)
  waiting for transfers between devices: 70.2 us -> 311 us
  between operations: 15 us -> 1.46 us
  matrix products: 25.7 us -> 33.9 us
  other arithmetic: 19.1 us -> 11.8 us
    ppermute x2, waiting for transfers between devices: 0.01 us -> 268 us  [extended(): lax.ppermute(lax.slice_in_dim(block, 0, width, axis=dim), axis, backward)]
    all_gather x1 -> x0, waiting for transfers between devices: 42 us -> none  [gather_weights(): lax.all_gather(jnp.concatenate([qkv_weight, out_wide], axis=1), 'tensor',...]
    all_to_all x1, waiting for transfers between devices: 9.75 us -> 25.1 us  [local(): lax.all_to_all(outgoing, 'dp', split_axis=0, concat_axis=0, tiled=True)]
    all_to_all x0 -> x1, starting transfers between devices: none -> 10.1 us  [gather_weights(): lax.all_to_all(jnp.stack([jnp.concatenate([qkv_weight, out_wide], axis=1)...]
    another operation x0 -> x1, local copies, waits for them, and re-layouts: none -> 5.88 us  [gather_weights(): jnp.stack([jnp.concatenate([qkv_weight, out_wide], axis=1)] * lax.axis_si...]
    dot_general x2, matrix products: 2.07 us -> 6.77 us  [times_out_t(): lax.dot_general(grad_rows[:, side * half:(side + 1) * half], out_pairs, (...]
    all_to_all x1, starting transfers between devices: 9.91 us -> 5.57 us  [local(): lax.all_to_all(back_slots, 'dp', split_axis=0, concat_axis=0, tiled=True)]
  transfers between devices with their start and end apart: 9 -> 9, of which waited for: 5 -> 6; matrix products, arithmetic and copies ran while one was open for 19% -> 7% of each run, Pallas kernels for 0% -> 0%
where the time goes in v1:
time: 421 us; the launch traced here: 420 us
  waiting for transfers between devices  311 us (74%)
  starting transfers between devices  41.8 us (10%)
  matrix products  33.9 us (8%)
  local copies, waits for them, and re-layouts  19.2 us (5%)
  other arithmetic  11.8 us (3%)
    ppermute x2, waiting for transfers between devices, extended(): lax.ppermute(lax.slice_in_dim(block, 0, width, axis=dim), axis, backward)  268 us
    all_to_all x1, waiting for transfers between devices, local(): lax.all_to_all(outgoing, 'dp', split_axis=0, concat_axis=0, tiled=True)  25.1 us
    all_to_all x1, waiting for transfers between devices, local(): lax.all_to_all(back_slots, 'dp', split_axis=0, concat_axis=0, tiled=True)  11.8 us
    all_to_all x1, starting transfers between devices, local(): lax.all_to_all(outgoing, 'dp', split_axis=0, concat_axis=0, tiled=True)  10.2 us
    all_to_all x1, starting transfers between devices, gather_weights(): lax.all_to_all(jnp.stack([jnp.concatenate([qkv_weight, out_wide], axis=1)...  10.1 us
  transfers between devices with their start and end apart: 9, of which 6 were waited for; matrix products, arithmetic and copies ran while one was open for 7% of the time, Pallas kernels for 0%

profile of v1, /device:TPU:66, one launch (start us, length us, event | category | flops | bytes accessed | tf_op | source)
XLA Modules:
  0.0 419.6 jit_solution(15050894225258487924)
XLA Ops:
  0.6 0.8 copy.21
  1.8 1.1 gather_fusion.1
  3.0 1.2 reshape.395
  4.2 10.2 %all-to-all-start = ((bf16[32,6,1792]{2,1,0:T(8,128)(2,1)}), bf16[32,6,1792]{2,1,0:T(8,128)(2,1)S(1)}, u32[]{:S(2)}, u32[]{:S(2)}) async-start(bf16[32,6,1792]{2,1,0:T(8,128)(2,1)} %reshape.395), calls=%async_computation | async-start | bytes 1835008 | tf_op jit(solution)/shard_map/all_to_all | solution.py:134
  14.6 25.1 %all-to-all-done = bf16[32,6,1792]{2,1,0:T(8,128)(2,1)S(1)} async-done(((bf16[32,6,1792]{2,1,0:T(8,128)(2,1)}), bf16[32,6,1792]{2,1,0:T(8,128)(2,1)S(1)}, u32[]{:S(2)}, u32[]{:S(2)}) %all-to-all-start) | async-done | bytes 688160 | tf_op jit(solution)/shard_map/all_to_all | solution.py:134
  39.7 5.9 %stack.6 = bf16[16,112,3584]{2,1,0:T(8,128)(2,1)} broadcast(bf16[112,3584]{1,0:T(8,128)(2,1)S(1)} %pad_maximum_fusion.1), dimensions={1,2} | broadcast | bytes 13647872 | tf_op jit(solution)/shard_map/stack | solution.py:30
  45.6 10.1 %all-to-all-start.1 = ((bf16[16,112,3584]{2,1,0:T(8,128)(2,1)}), bf16[16,112,3584]{2,1,0:T(8,128)(2,1)}, u32[]{:S(2)}, u32[]{:S(2)}) async-start(bf16[16,112,3584]{2,1,0:T(8,128)(2,1)} %stack.6), calls=%async_computation.1 | async-start | bytes 25690112 | tf_op jit(solution)/shard_map/all_to_all | solution.py:29
  55.8 2.0 collective-permute-start.1
  57.8 2.3 collective-permute-start
  60.3 1.2 scatter_custom_fusion.1
  61.6 0.5 copy-done.17
  62.2 0.5 compare_and_fusion
  62.8 0.8 copy.28
  63.6 0.8 copy.27
  64.5 267.7 %collective-permute-done.1 = s32[96]{0:T(128)S(1)} collective-permute-done((s32[96]{0:T(128)S(1)}, s32[96]{0:T(128)S(1)}, u32[]{:S(2)}, u32[]{:S(2)}) %collective-permute-start.1) | collective-permute-done | bytes 416 | tf_op jit(solution)/shard_map/ppermute | solution.py:19
  332.3 0.5 collective-permute-done
  333.2 0.9 gather_fusion
  334.7 5.4 %fusion.9 = bf16[128,2688]{1,0:T(8,128)(2,1)S(1)} fusion(bf16[1792,3584]{1,0:T(8,128)(2,1)} %bitcast.8, f32[1792]{0:T(1024)S(1)} %copy-done.20, f32[128]{0:T(128)S(1)} %add_rsqrt_fusion, f32[128]{0:T(128)S(1)} %broadcast_multiply_fusion.2, bf16[128,1792]{1,0:T(8,128)(2,1)S(1)} %gather_fusion, pred[128]{0:T(512)(128)(4,1)S(1)} %compare_and_fusion.2), kind=kOutput, calls=%fused_computation.15 | convolution fusion | flops 1234845696 | bytes 10788992 | tf_op jit(solution)/shard_map/dot_general | solution.py:147
  340.2 3.8 collective-permute-start.3
  344.0 2.1 collective-permute-start.2
  346.1 2.9 convolution_bitcast_fusion.1
  349.0 3.9 fusion.12
  352.9 1.2 reduce_sum.76
  354.3 1.1 fusion.18
  355.7 1.0 fusion.109
  356.8 0.9 multiply_reduce_fusion
  357.8 0.9 fusion.79
  358.7 0.3 multiply_convert_fusion
  359.0 0.8 fusion.110
  360.0 3.7 collective-permute-start.4
  363.7 2.0 collective-permute-start.5
  365.9 1.7 fusion.37
  367.6 4.7 %collective-permute-done.4 = f32[96,1792]{1,0:T(8,128)S(1)} collective-permute-done((f32[96,1792]{1,0:T(8,128)S(1)}, f32[96,1792]{1,0:T(8,128)S(1)}, u32[]{:S(2)}, u32[]{:S(2)}) %collective-permute-start.4) | collective-permute-done | bytes 688160 | tf_op jit(solution)/shard_map/ppermute | solution.py:180
  372.5 1.7 collective-permute-done.5
  374.4 7.4 %fusion.106 = (f32[128]{0:T(128)S(1)}, f32[128]{0:T(128)S(1)}, f32[128,1792]{1,0:T(8,128)}) fusion(f32[128]{0:T(128)S(1)} %copy-done.19, f32[128]{0:T(128)S(1)} %copy-done.11, bf16[128,1792]{1,0:T(8,128)(2,1)S(1)} %gather_fusion, pred[128]{0:T(512)(128)(4,1)S(1)} %compare_and_fusion.2, f32[1792]{0:T(1024)S(1)} %copy-done.21, ...), kind=kOutput, calls=%fused_computation.154 | convolution fusion | flops 1236336384 | bytes 11707520 | tf_op jit(solution)/shard_map/dot_general | solution.py:185
  381.8 2.7 scatter_custom_fusion
  384.6 1.2 reshape.404
  385.8 5.6 %all-to-all-start.2 = ((bf16[32,6,1792]{2,1,0:T(8,128)(2,1)}), bf16[32,6,1792]{2,1,0:T(8,128)(2,1)S(1)}, u32[]{:S(2)}, u32[]{:S(2)}) async-start(bf16[32,6,1792]{2,1,0:T(8,128)(2,1)} %reshape.404), calls=%async_computation.2 | async-start | bytes 1835008 | tf_op jit(solution)/shard_map/all_to_all | solution.py:199
  391.4 3.8 fusion.19
  395.2 2.2 reduce_sum.75
  397.4 0.8 copy.29
  398.2 1.1 fusion.108
  399.3 2.6 fusion.31
  401.9 2.6 fusion.28
  404.5 1.0 fusion.55
  405.5 11.8 %all-to-all-done.2 = bf16[32,6,1792]{2,1,0:T(8,128)(2,1)S(1)} async-done(((bf16[32,6,1792]{2,1,0:T(8,128)(2,1)}), bf16[32,6,1792]{2,1,0:T(8,128)(2,1)S(1)}, u32[]{:S(2)}, u32[]{:S(2)}) %all-to-all-start.2) | async-done | bytes 688160 | tf_op jit(solution)/shard_map/all_to_all | solution.py:199
  417.5 1.1 gather_fusion.2
  418.7 1.0 select_bitcast_fusion
  (104 shorter events, 3.5 us)
Async XLA Ops:
  0.6 1.1 copy-start
  3.0 11.4 %copy-start.7 = (bf16[56,1792]{1,0:T(8,128)(2,1)S(1)}, bf16[56,1792]{1,0:T(8,128)(2,1)}, u32[]{:S(2)}) copy-start(bf16[56,1792]{1,0:T(8,128)(2,1)} %param.20) | copy-start | bytes 602116
  3.0 11.5 %copy-start.4 = (bf16[112,2688]{1,0:T(8,128)(2,1)S(1)}, bf16[112,2688]{1,0:T(8,128)(2,1)}, u32[]{:S(2)}) copy-start(bf16[112,2688]{1,0:T(8,128)(2,1)} %param.19) | copy-start | bytes 1806340
  4.2 35.5 %all-to-all-start = ((bf16[32,6,1792]{2,1,0:T(8,128)(2,1)}), bf16[32,6,1792]{2,1,0:T(8,128)(2,1)S(1)}, u32[]{:S(2)}, u32[]{:S(2)}) async-start(bf16[32,6,1792]{2,1,0:T(8,128)(2,1)} %reshape.395), calls=%async_computation | async-start | bytes 1835008 | tf_op jit(solution)/shard_map/all_to_all | solution.py:134
  45.6 10.1 %copy-start.22 = (s32[1,128]{1,0:T(1,128)S(1)}, s32[1,128]{1,0:T(1,128)}, u32[]{:S(2)}) copy-start(s32[1,128]{1,0:T(1,128)} %param.17) | copy-start | bytes 1540
  45.6 15.9 %copy-start.23 = (s32[1,128]{1,0:T(1,128)S(1)}, s32[1,128]{1,0:T(1,128)}, u32[]{:S(2)}) copy-start(s32[1,128]{1,0:T(1,128)} %param.16) | copy-start | bytes 1540
  45.6 289.1 %all-to-all-start.1 = ((bf16[16,112,3584]{2,1,0:T(8,128)(2,1)}), bf16[16,112,3584]{2,1,0:T(8,128)(2,1)}, u32[]{:S(2)}, u32[]{:S(2)}) async-start(bf16[16,112,3584]{2,1,0:T(8,128)(2,1)} %stack.6), calls=%async_computation.1 | async-start | bytes 25690112 | tf_op jit(solution)/shard_map/all_to_all | solution.py:29
  55.8 276.4 %collective-permute-start.1 = (s32[96]{0:T(128)S(1)}, s32[96]{0:T(128)S(1)}, u32[]{:S(2)}, u32[]{:S(2)}) collective-permute-start(s32[96]{0:T(128)S(1)} %get-tuple-element.42), channel_id=1, source_target_pairs={{1,0},{2,1},{3,2},{4,3},{5,4},{6,5},{7,6},{8,7},{9,8},{10,9},{11,1... | collective-permute-start | bytes 1160 | tf_op jit(solution)/shard_map/ppermute | solution.py:19
  57.8 274.9 %collective-permute-start = (s32[96]{0:T(128)S(1)}, s32[96]{0:T(128)S(1)}, u32[]{:S(2)}, u32[]{:S(2)}) collective-permute-start(s32[96]{0:T(128)S(1)} %get-tuple-element.41), channel_id=1, source_target_pairs={{0,1},{1,2},{2,3},{3,4},{4,5},{5,6},{6,7},{7,8},{8,9},{9,10},{10,1... | collective-permute-start | bytes 1160 | tf_op jit(solution)/shard_map/ppermute | solution.py:16
  61.5 292.8 %copy-start.12 = (pred[1024]{0:T(1024)(128)(4,1)}, pred[1024]{0:T(1024)(128)(4,1)S(1)}, u32[]{:S(2)}) copy-start(pred[1024]{0:T(1024)(128)(4,1)S(1)} %fusion.95) | copy-start | bytes 3076
  61.6 0.5 copy-start.17
  62.8 291.5 %copy-start.14 = (pred[896]{0:T(1024)(128)(4,1)}, pred[896]{0:T(1024)(128)(4,1)S(1)}, u32[]{:S(2)}) copy-start(pred[896]{0:T(1024)(128)(4,1)S(1)} %fusion.94) | copy-start | bytes 2692
  333.2 1.5 copy-start.20
  334.4 5.7 %copy-start.10 = (f32[128]{0:T(128)}, f32[128]{0:T(128)S(1)}, u32[]{:S(2)}) copy-start(f32[128]{0:T(128)S(1)} %broadcast_multiply_fusion.2) | copy-start | bytes 1540
  334.7 5.4 %copy-start.18 = (f32[128]{0:T(128)}, f32[128]{0:T(128)S(1)}, u32[]{:S(2)}) copy-start(f32[128]{0:T(128)S(1)} %add_rsqrt_fusion) | copy-start | bytes 1540
  340.1 8.9 %copy-start.2 = (bf16[128,2688]{1,0:T(8,128)(2,1)}, bf16[128,2688]{1,0:T(8,128)(2,1)S(1)}, u32[]{:S(2)}) copy-start(bf16[128,2688]{1,0:T(8,128)(2,1)S(1)} %fusion.9) | copy-start | bytes 2064388
  340.2 5.9 %copy-start.5 = (bf16[1,128,1792]{2,1,0:T(8,128)(2,1)S(1)}, bf16[1,128,1792]{2,1,0:T(8,128)(2,1)}, u32[]{:S(2)}) copy-start(bf16[1,128,1792]{2,1,0:T(8,128)(2,1)} %param.21) | copy-start | bytes 1376260
  340.2 15.2 %collective-permute-start.3 = (bf16[96,1792]{1,0:T(8,128)(2,1)S(1)}, bf16[96,1792]{1,0:T(8,128)(2,1)S(1)}, u32[]{:S(2)}, u32[]{:S(2)}) collective-permute-start(bf16[96,1792]{1,0:T(8,128)(2,1)S(1)} %get-tuple-element.36), channel_id=1, source_target_pairs={{1,0},{2,1},{3,2},{4,3},{5,4},{6,5},{7,6},{8,7},{9,8},{10,9},{11,1... | collective-permute-start | bytes 1032200 | tf_op jit(solution)/shard_map/ppermute | solution.py:19
  344.0 11.4 %collective-permute-start.2 = (bf16[96,1792]{1,0:T(8,128)(2,1)S(1)}, bf16[96,1792]{1,0:T(8,128)(2,1)S(1)}, u32[]{:S(2)}, u32[]{:S(2)}) collective-permute-start(bf16[96,1792]{1,0:T(8,128)(2,1)S(1)} %get-tuple-element.35), channel_id=1, source_target_pairs={{0,1},{1,2},{2,3},{3,4},{4,5},{5,6},{6,7},{7,8},{8,9},{9,10},{10,1... | collective-permute-start | bytes 1032200 | tf_op jit(solution)/shard_map/ppermute | solution.py:16
  349.0 5.3 %slice-start.1 = ((bf16[128,2688]{1,0:T(8,128)(2,1)}), bf16[128,896]{1,0:T(8,128)(2,1)S(1)}, s32[]{:S(2)}) async-start(bf16[128,2688]{1,0:T(8,128)(2,1)} %copy-done.2), calls=%async_computation.4 | async-start | bytes 458752 | tf_op jit(solution)/shard_map/slice | solution.py:148
  354.3 1.1 slice-start
  355.5 3.1 copy-start.3
  359.8 6.0 %slice-start.2 = ((bf16[320,1792]{1,0:T(8,128)(2,1)}), bf16[320,896]{1,0:T(8,128)(2,1)S(1)}, s32[]{:S(2)}) async-start(bf16[320,1792]{1,0:T(8,128)(2,1)} %copy-done.3), calls=%async_computation.5 | async-start | bytes 1146880 | tf_op jit(solution)/shard_map/slice | solution.py:108
  359.9 6.0 %copy-start.8 = (s32[8,320]{0,1:T(8,128)S(1)}, s32[8,320]{0,1:T(8,128)}, u32[]{:S(2)}) copy-start(s32[8,320]{0,1:T(8,128)} %copy.28) | copy-start | bytes 30724
  359.9 6.0 %copy-start.9 = (s32[8,320]{0,1:T(8,128)S(1)}, s32[8,320]{0,1:T(8,128)}, u32[]{:S(2)}) copy-start(s32[8,320]{0,1:T(8,128)} %copy.27) | copy-start | bytes 30724
  359.9 6.0 %copy-start.15 = (pred[896]{0:T(1024)(128)(4,1)S(1)}, pred[896]{0:T(1024)(128)(4,1)}, u32[]{:S(2)}) copy-start(pred[896]{0:T(1024)(128)(4,1)} %copy-done.14) | copy-start | bytes 2692
  360.0 12.4 %collective-permute-start.4 = (f32[96,1792]{1,0:T(8,128)S(1)}, f32[96,1792]{1,0:T(8,128)S(1)}, u32[]{:S(2)}, u32[]{:S(2)}) collective-permute-start(f32[96,1792]{1,0:T(8,128)S(1)} %get-tuple-element.29), channel_id=1, source_target_pairs={{0,1},{1,2},{2,3},{3,4},{4,5},{5,6},{6,7},{7,8},{8,9},{9,10},{10,1... | collective-permute-start | bytes 2064392 | tf_op jit(solution)/shard_map/ppermute | solution.py:180
  363.7 10.5 %collective-permute-start.5 = (f32[96,1792]{1,0:T(8,128)S(1)}, f32[96,1792]{1,0:T(8,128)S(1)}, u32[]{:S(2)}, u32[]{:S(2)}) collective-permute-start(f32[96,1792]{1,0:T(8,128)S(1)} %get-tuple-element.30), channel_id=1, source_target_pairs={{1,0},{2,1},{3,2},{4,3},{5,4},{6,5},{7,6},{8,7},{9,8},{10,9},{11,1... | collective-permute-start | bytes 2064392 | tf_op jit(solution)/shard_map/ppermute | solution.py:181
  372.5 1.9 copy-start.11
  372.5 1.9 copy-start.19
  372.5 1.9 copy-start.21
  374.4 7.5 %copy-start.6 = (bf16[1,128,1792]{2,1,0:T(8,128)(2,1)S(1)}, bf16[1,128,1792]{2,1,0:T(8,128)(2,1)}, u32[]{:S(2)}) copy-start(bf16[1,128,1792]{2,1,0:T(8,128)(2,1)} %param.21) | copy-start | bytes 1376260
  384.6 6.8 %copy-start.13 = (pred[1024]{0:T(1024)(128)(4,1)S(1)}, pred[1024]{0:T(1024)(128)(4,1)}, u32[]{:S(2)}) copy-start(pred[1024]{0:T(1024)(128)(4,1)} %copy-done.12) | copy-start | bytes 3076
  385.8 31.5 %all-to-all-start.2 = ((bf16[32,6,1792]{2,1,0:T(8,128)(2,1)}), bf16[32,6,1792]{2,1,0:T(8,128)(2,1)S(1)}, u32[]{:S(2)}, u32[]{:S(2)}) async-start(bf16[32,6,1792]{2,1,0:T(8,128)(2,1)} %reshape.404), calls=%async_computation.2 | async-start | bytes 1835008 | tf_op jit(solution)/shard_map/all_to_all | solution.py:199
  417.5 1.2 copy-start.16
  417.5 2.1 copy-start.1
